TPU v7x, 32 devices: a whole 2x2x4 slice. The times are simulated.
32 devices in a mesh: day: 4 (over z), dom: 8 (over y, x, core).
Axes of the slice: x: 2, y: 2, z: 4, core: 2. Of those that a mesh axis runs over, the one named last changes fastest.
Arguments:
- node_states: bfloat16 [16, 2048, 256], P('day', 'dom'), may hold values from -12 to 12
- edge_source: int32 [16, 8192], P('day', 'dom'), may hold values from 0 to 383
- edge_target: int32 [16, 8192], P('day', 'dom'), may hold values from 0 to 255
- halo_rows: int32 [16, 1024], P('day', 'dom'), may hold values from 0 to 255
- halo_count: int32 [16, 8], P('day', 'dom'), may hold values from 1 to 128, 640 in all within a row
- w_message: bfloat16 [256, 256], replicated, may hold values from -0.375 to 0.375
- w_query: bfloat16 [256, 256], replicated, may hold values from -1 to 1, as said below
- w_key: bfloat16 [256, 256], replicated, may hold values from -1 to 1, as said below
- w_value: bfloat16 [256, 256], replicated, may hold values from -0.375 to 0.375
- cotangent: bfloat16 [16, 8, 4, 64, 256], P(None, 'dom', 'day'), may hold values from -6 to 6
Outputs:
- state_grad: float32 [16, 2048, 256], P('day', 'dom')
- grad_message: float32 [256, 256], replicated
- grad_query: float32 [256, 256], replicated
- grad_key: float32 [256, 256], replicated
- grad_value: float32 [256, 256], replicated
Inputs may be any that keep to these rules, and one draw needn't show every extreme that they name: `edge_source`: indices of the extended rows: below 256 a partition's own account, from 256 on a received halo slot. `halo_rows`: rows of the sending partition's own block; repeats allowed. `halo_count`: on every day some partition has all 128 slots live. `w_query`: entries of order 256 ** -0.5. `w_key`: entries of order 256 ** -0.5.
All inputs are finite; a program needn't handle non-finite values. No bound on the sum of `halo_count` on one device may be relied on, other than what follows from the above.
Results may differ from a plain program's by a relative error of at most 0.004.
The roundings to bfloat16 on the way count: a program that leaves them out, or rounds other values in their place, can miss the bound.
Values may be sent and summed in bfloat16 or wider, within the bound.
No kernel may reach another device: no remote copies, remote signals or barrier semaphores. Data moves between devices by JAX's collectives and lax.ppermute only.
A program may use at most 64 MiB of HBM per device.

v0:
```python
import jax
import jax.numpy as jnp
from jax import lax
from jax.sharding import PartitionSpec as P

HEADS = 4


def from_behind(value, axis, steps):
    count = lax.axis_size(axis)
    pairs = [(source, (source + steps) % count) for source in range(count)]
    return lax.ppermute(value, axis, pairs)


def _power_of_two(count):
    return count > 0 and count & count - 1 == 0


def tree_sum(values, axes):
    sizes = [lax.axis_size(axis) for axis in axes]
    flat = jnp.concatenate([value.reshape(-1) for value in values])
    total = 1
    for size in sizes:
        total *= size
    if not all((_power_of_two(size) for size in sizes)) or flat.shape[0] % total:
        return lax.psum(tuple(values), axes)
    steps = [
        (axis, bit)
        for axis, size in zip(axes, sizes)
        for bit in [1 << k for k in range(size.bit_length() - 1)]
    ]
    for axis, bit in steps:
        side = lax.axis_index(axis) // bit % 2
        halves = flat.reshape(2, -1)
        keep = jnp.where(side == 0, halves[0], halves[1])
        send = jnp.where(side == 0, halves[1], halves[0])
        pairs = [(source, source ^ bit) for source in range(lax.axis_size(axis))]
        flat = keep + lax.ppermute(send, axis, pairs)
    for axis, bit in reversed(steps):
        side = lax.axis_index(axis) // bit % 2
        pairs = [(source, source ^ bit) for source in range(lax.axis_size(axis))]
        other = lax.ppermute(flat, axis, pairs)
        flat = jnp.where(side == 0, jnp.concatenate([flat, other]), jnp.concatenate([other, flat]))
    results, start = ([], 0)
    for value in values:
        results.append(flat[start : start + value.size].reshape(value.shape))
        start += value.size
    return tuple(results)


def adjacency(sources, targets, count_rows, total_rows):
    target_hot = (targets[:, None] == jnp.arange(count_rows, dtype=jnp.int32)[None, :]).astype(
        jnp.bfloat16
    )
    source_hot = (sources[:, None] == jnp.arange(total_rows, dtype=jnp.int32)[None, :]).astype(
        jnp.bfloat16
    )
    counts = lax.dot_general(
        target_hot, source_hot, (((0,), (0,)), ((), ())), preferred_element_type=jnp.float32
    )
    return counts.astype(jnp.bfloat16)


def gnn_forward(states, received, adjacent, w_message):
    extended = jnp.concatenate([states, received], axis=0)
    neighbours = jnp.dot(adjacent, extended, preferred_element_type=jnp.float32)
    counted = jnp.sum(adjacent.astype(jnp.float32), axis=1)
    inverse = 1.0 / (counted + 1.0)
    aggregate = ((states.astype(jnp.float32) + neighbours) * inverse[:, None]).astype(jnp.bfloat16)
    preact = jnp.dot(aggregate, w_message, preferred_element_type=jnp.float32)
    hidden = (states.astype(jnp.float32) + jax.nn.silu(preact)).astype(jnp.bfloat16)
    return (aggregate, preact, inverse, hidden)


def gnn_backward(upstream, aggregate, preact, inverse, adjacent, w_message):
    count_rows = aggregate.shape[0]
    up_float = upstream.astype(jnp.float32)
    sigmoid_val = jax.nn.sigmoid(preact)
    pre_grad = (up_float * sigmoid_val * (1.0 + preact * (1.0 - sigmoid_val))).astype(jnp.bfloat16)
    message_part = lax.dot_general(
        aggregate, pre_grad, (((0,), (0,)), ((), ())), preferred_element_type=jnp.float32
    )
    agg_grad = lax.dot_general(
        pre_grad, w_message, (((1,), (1,)), ((), ())), preferred_element_type=jnp.float32
    )
    term_grad = agg_grad * inverse[:, None]
    ext_grad = lax.dot_general(
        adjacent.astype(jnp.float32),
        term_grad,
        (((0,), (0,)), ((), ())),
        precision=lax.Precision.HIGHEST,
        preferred_element_type=jnp.float32,
    )
    local_grad = up_float + term_grad + ext_grad[:count_rows]
    halo_grad = ext_grad[count_rows:].astype(jnp.bfloat16)
    return (message_part, local_grad, halo_grad)


def attend(states, upstream, w_query, w_key, w_value):
    steps_all, nodes_here, width = states.shape
    head_dim = width // HEADS
    scale_factor = head_dim ** (-0.5)
    flat = states.reshape(steps_all * nodes_here, width)

    def project(weight):
        return jnp.dot(flat, weight, preferred_element_type=jnp.float32).astype(jnp.bfloat16)

    def splitter(matrix):
        return matrix.reshape(steps_all, nodes_here, HEADS, head_dim).astype(jnp.float32)

    queries = project(w_query)
    key_rows = project(w_key)
    value_rows = project(w_value)
    query_f = splitter(queries)
    key_f = splitter(key_rows)
    value_f = splitter(value_rows)
    scores = jnp.einsum("tnhd,snhd->nhts", query_f, key_f) * scale_factor
    causal = jnp.arange(steps_all)[:, None] >= jnp.arange(steps_all)[None, :]
    scores = jnp.where(causal, scores, -jnp.inf)
    highest = jnp.max(scores, axis=-1, keepdims=True)
    exponent = jnp.exp(scores - highest)
    probs = exponent / jnp.sum(exponent, axis=-1, keepdims=True)
    probs_low = probs.astype(jnp.bfloat16).astype(jnp.float32)
    up_heads = splitter(upstream)
    value_grad = jnp.einsum("nhts,tnhd->snhd", probs_low, up_heads).astype(jnp.bfloat16)
    prob_grad = jnp.einsum("tnhd,snhd->nhts", up_heads, value_f)
    score_grad = (
        probs * (prob_grad - jnp.sum(prob_grad * probs, axis=-1, keepdims=True)) * scale_factor
    ).astype(jnp.bfloat16)
    score_f = score_grad.astype(jnp.float32)
    query_grad = jnp.einsum("nhts,snhd->tnhd", score_f, key_f).astype(jnp.bfloat16)
    key_grad = jnp.einsum("nhts,tnhd->snhd", score_f, query_f).astype(jnp.bfloat16)
    query_flat = query_grad.reshape(steps_all * nodes_here, width)
    key_flat = key_grad.reshape(steps_all * nodes_here, width)
    value_flat = value_grad.reshape(steps_all * nodes_here, width)

    def weight_grad(grad_rows):
        return lax.dot_general(
            flat, grad_rows, (((0,), (0,)), ((), ())), preferred_element_type=jnp.float32
        )

    def input_grad(grad_rows, weight):
        return lax.dot_general(
            grad_rows, weight, (((1,), (1,)), ((), ())), preferred_element_type=jnp.float32
        )

    back = upstream.reshape(steps_all * nodes_here, width).astype(jnp.float32)
    back = (
        back
        + input_grad(query_flat, w_query)
        + input_grad(key_flat, w_key)
        + input_grad(value_flat, w_value)
    )
    back = back.astype(jnp.bfloat16).reshape(steps_all, nodes_here, width)
    return ((weight_grad(query_flat), weight_grad(key_flat), weight_grad(value_flat)), back)


def local(
    node_states,
    edge_source,
    edge_target,
    halo_rows,
    halo_count,
    w_message,
    w_query,
    w_key,
    w_value,
    cotangent,
):
    days_local, node_local, width = node_states.shape
    halo_slots = halo_rows.shape[1]
    live = jnp.arange(halo_slots)[None, :] < halo_count
    picked = jnp.take_along_axis(node_states, halo_rows[:, :, None], axis=1)
    sent = jnp.where(live[:, :, None], picked, jnp.zeros_like(picked))
    received = from_behind(sent, "dom", 1)

    def forward_one(items):
        adjacent = adjacency(items[2], items[3], node_local, node_local + halo_slots)
        aggregate, preact, inverse, hidden = gnn_forward(items[0], items[1], adjacent, w_message)
        return (aggregate, preact, inverse, hidden, adjacent)

    aggregate, preact, inverse, hidden, adjacent = lax.map(
        forward_one, (node_states, received, edge_source, edge_target)
    )
    node_major = lax.all_to_all(hidden, "day", split_axis=1, concat_axis=0, tiled=True)
    upstream = cotangent.reshape(cotangent.shape[0], -1, width)
    attn_grads, back = attend(node_major, upstream, w_query, w_key, w_value)
    back_days = lax.all_to_all(back, "day", split_axis=0, concat_axis=1, tiled=True)

    def backward_one(items):
        return gnn_backward(items[0], items[1], items[2], items[3], items[4], w_message)

    message_parts, local_grad, halo_grad = lax.map(
        backward_one, (back_days, aggregate, preact, inverse, adjacent)
    )
    grad_message = jnp.sum(message_parts, axis=0)
    returned = from_behind(halo_grad, "dom", -1)
    slot_hot = jnp.logical_and(
        halo_rows[:, :, None] == jnp.arange(node_local, dtype=jnp.int32)[None, None, :],
        live[:, :, None],
    ).astype(jnp.bfloat16)
    scattered = jnp.einsum("dsn,dsh->dnh", slot_hot, returned, preferred_element_type=jnp.float32)
    state_grad = local_grad + scattered
    grad_message, grad_query, grad_key, grad_value = tree_sum(
        (grad_message, attn_grads[0], attn_grads[1], attn_grads[2]), ("dom", "day")
    )
    return (state_grad, grad_message, grad_query, grad_key, grad_value)


def solution(mesh):
    return jax.shard_map(
        local,
        mesh=mesh,
        in_specs=(
            P("day", "dom", None),
            P("day", "dom"),
            P("day", "dom"),
            P("day", "dom"),
            P("day", "dom"),
            P(),
            P(),
            P(),
            P(),
            P(None, "dom", "day", None, None),
        ),
        out_specs=(P("day", "dom", None), P(), P(), P(), P()),
        check_vma=False,
    )
```

profile of v0, /device:TPU:1, one launch (start us, length us, event | category | flops | bytes accessed | tf_op | source)
XLA Modules:
  0.0 185.2 jit_solution(11964779627345640827)
XLA Ops:
  2.1 7.0 %gather_fusion = bf16[512,256]{1,0:T(8,128)(2,1)S(1)} fusion(bf16[4,256,256]{2,1,0:T(8,128)(2,1)} %param.14, s32[512]{0:T(512)S(1)} %fusion.70), kind=kCustom, calls=%fused_computation | custom fusion | bytes 528384 | tf_op jit(solution)/shard_map/jit(take_along_axis)/gather | solution.py:173
  9.4 2.7 %collective-permute-start = (bf16[4,128,256]{2,1,0:T(8,128)(2,1)S(1)}, bf16[4,128,256]{2,1,0:T(8,128)(2,1)S(1)}, u32[]{:S(2)}, u32[]{:S(2)}) collective-permute-start(bf16[4,128,256]{2,1,0:T(8,128)(2,1)S(1)} %select_select_fusion), channel_id=1, source_target_pairs={{0,1},{1,2},{2,3},{3,4},{4,5},{5,6},{6,7},{7,0},{8,9},{9,10},{10,1... | collective-permute-start | bytes 786440 | tf_op jit(solution)/shard_map/ppermute | solution.py:12
  12.0 3.3 %collective-permute-done = bf16[4,128,256]{2,1,0:T(8,128)(2,1)S(1)} collective-permute-done((bf16[4,128,256]{2,1,0:T(8,128)(2,1)S(1)}, bf16[4,128,256]{2,1,0:T(8,128)(2,1)S(1)}, u32[]{:S(2)}, u32[]{:S(2)}) %collective-permute-start) | collective-permute-done | bytes 262176 | tf_op jit(solution)/shard_map/ppermute | solution.py:12
  15.4 14.8 %while.34 = (s32[]{:T(128)}, bf16[4,256,256]{2,1,0:T(8,128)(2,1)}, f32[4,256,256]{2,1,0:T(8,128)S(1)}, f32[4,256]{1,0:T(4,128)S(1)}, bf16[4,256,256]{2,1,0:T(8,1...) while((s32[]{:T(128)}, bf16[4,256,256]{2,1,0:T(8,128)(2,1)}, ...), condition=%wide.region_2.3_spmd.clone, body=%wide.region_0.2_spmd.sunk.clone | while | flops 287277312 | bytes 3112069 | solution.py:182
  30.2 1.2 copy.52
  31.4 4.6 %all-to-all-start = ((bf16[4,256,256]{2,0,1:T(4,128)(2,1)}), bf16[4,256,256]{2,0,1:T(4,128)(2,1)S(1)}, u32[]{:S(2)}, u32[]{:S(2)}) async-start(bf16[4,256,256]{2,0,1:T(4,128)(2,1)} %copy.52), calls=%async_computation | async-start | bytes 1048576 | tf_op jit(solution)/shard_map/all_to_all | solution.py:185
  36.5 12.6 %all-to-all-done = bf16[4,256,256]{2,0,1:T(4,128)(2,1)S(1)} async-done(((bf16[4,256,256]{2,0,1:T(4,128)(2,1)}), bf16[4,256,256]{2,0,1:T(4,128)(2,1)S(1)}, u32[]{:S(2)}, u32[]{:S(2)}) %all-to-all-start) | async-done | bytes 524320 | tf_op jit(solution)/shard_map/all_to_all | solution.py:185
  49.5 1.4 reshape.172
  51.2 1.4 reshape.173
  53.7 2.0 %reshape.174 = bf16[16,64,4,64]{3,2,1,0:T(4,128)(2,1)S(1)} reshape(bf16[1024,256]{1,0:T(8,128)(2,1)} %convolution_convert_fusion.3) | data formatting | bytes 1048576 | tf_op jit(solution)/shard_map/reshape | solution.py:109
  55.8 2.6 %fusion.52 = f32[64,4,16,16]{3,2,1,0:T(8,128)} fusion(bf16[16,64,4,64]{3,2,1,0:T(4,128)(2,1)S(1)} %reshape.174, bf16[16,64,4,64]{3,2,1,0:T(4,128)(2,1)S(1)} %reshape_reshape.4), kind=kOutput, calls=%fused_computation.91 | convolution fusion | flops 8388608 | bytes 1310720 | tf_op jit(solution)/shard_map/tnhd,snhd->nhts/dot_general | solution.py:126
  58.3 5.5 %fusion.78 = (f32[64,4,16]{2,1,0:T(4,128)}, f32[64,4,16,16]{2,3,1,0:T(8,128)}) fusion(pred[16,16]{0,1:T(8,128)(4,1)S(1)} %iota_compare_fusion.7, bf16[16,64,4,64]{3,2,1,0:T(4,128)(2,1)} %reshape.172, bf16[16,64,4,64]{3,2,1,0:T(4,128)(2,1)} %reshape.173), kind=kOutput, calls=%fused_computation.145 | convolution fusion | flops 8650767 | bytes 1327360 | tf_op jit(solution)/shard_map/sub | solution.py:121
  63.9 6.2 %fusion.50 = bf16[16,64,4,64]{3,0,2,1:T(8,128)(2,1)} fusion(f32[64,4,16,16]{3,2,1,0:T(8,128)} %fusion.52, bf16[16,64,4,64]{3,2,1,0:T(4,128)(2,1)} %reshape.173, f32[64,4,16,16]{2,3,1,0:T(8,128)} %get-tuple-element.183, f32[64,4,16]{2,1,0:T(4,128)} %get-tuple-element.182), kind=kOutput, calls=%fused_computation.78 | convolution fusion | flops 9113615 | bytes 1589248 | tf_op jit(solution)/shard_map/nhts,tnhd->snhd/dot_general | solution.py:132
  70.0 5.9 %fusion.48 = bf16[16,64,4,64]{3,0,2,1:T(8,128)(2,1)} fusion(f32[64,4,16,16]{3,2,1,0:T(8,128)} %fusion.52, bf16[16,64,4,64]{3,2,1,0:T(4,128)(2,1)S(1)} %copy-done.6, f32[64,4,16,16]{2,3,1,0:T(8,128)} %get-tuple-element.183, f32[64,4,16]{2,1,0:T(4,128)} %get-tuple-element.182), kind=kOutput, calls=%fused_computation.76 | convolution fusion | flops 9113615 | bytes 1589248 | tf_op jit(solution)/shard_map/nhts,snhd->tnhd/dot_general | solution.py:131
  75.9 3.5 %fusion.49 = bf16[16,64,4,64]{3,0,2,1:T(8,128)(2,1)} fusion(bf16[16,64,4,64]{3,2,1,0:T(4,128)(2,1)S(1)} %reshape_reshape.4, f32[64,4,16,16]{2,3,1,0:T(8,128)} %get-tuple-element.183, f32[64,4,16]{2,1,0:T(4,128)} %get-tuple-element.182), kind=kOutput, calls=%fused_computation.77 | convolution fusion | flops 8781824 | bytes 1327104 | tf_op jit(solution)/shard_map/nhts,tnhd->snhd/dot_general | solution.py:125
  79.4 2.9 %copy.63 = bf16[16,64,4,64]{1,0,3,2:T(8,128)(2,1)S(1)} copy(bf16[16,64,4,64]{3,0,2,1:T(8,128)(2,1)} %fusion.50) | data formatting | bytes 1048576 | tf_op jit(solution)/shard_map/convert_element_type | solution.py:132
  83.0 3.1 %copy.61 = bf16[16,64,4,64]{1,0,3,2:T(8,128)(2,1)S(1)} copy(bf16[16,64,4,64]{3,0,2,1:T(8,128)(2,1)} %fusion.48) | data formatting | bytes 1048576 | tf_op jit(solution)/shard_map/convert_element_type | solution.py:131
  89.7 2.9 %copy.65 = bf16[16,64,4,64]{1,0,3,2:T(8,128)(2,1)S(1)} copy(bf16[16,64,4,64]{3,0,2,1:T(8,128)(2,1)} %fusion.49) | data formatting | bytes 1048576 | tf_op jit(solution)/shard_map/convert_element_type | solution.py:125
  94.9 3.5 %all-to-all-start.1 = ((bf16[16,64,256]{2,1,0:T(8,128)(2,1)}), bf16[16,64,256]{2,1,0:T(8,128)(2,1)S(1)}, u32[]{:S(2)}, u32[]{:S(2)}) async-start(bf16[16,64,256]{2,1,0:T(8,128)(2,1)} %bitcast.30), calls=%async_computation.1 | async-start | bytes 1048576 | tf_op jit(solution)/shard_map/all_to_all | solution.py:188
  99.5 12.0 %all-to-all-done.1 = bf16[16,64,256]{2,1,0:T(8,128)(2,1)S(1)} async-done(((bf16[16,64,256]{2,1,0:T(8,128)(2,1)}), bf16[16,64,256]{2,1,0:T(8,128)(2,1)S(1)}, u32[]{:S(2)}, u32[]{:S(2)}) %all-to-all-start.1) | async-done | bytes 524320 | tf_op jit(solution)/shard_map/all_to_all | solution.py:188
  111.8 18.2 %while.35 = (s32[]{:T(128)}, f32[4,256,256]{2,1,0:T(8,128)S(1)}, f32[4,256,256]{2,1,0:T(8,128)S(1)}, bf16[4,128,256]{2,1,0:T(8,128)(2,1)}, bf16[4,256,256]{2,1,0...) while((s32[]{:T(128)}, f32[4,256,256]{2,1,0:T(8,128)S(1)}, ...), condition=%wide.region_7.8_spmd.clone, body=%wide.region_6.7_spmd.sunk.clone | while | flops 370671616 | bytes 3479661 | solution.py:193
  111.8 1.2 convolution_multiply_fusion.3
  113.0 1.3 fusion.147
  115.0 1.3 fusion.146
  116.4 1.2 convolution_multiply_fusion.3
  117.6 1.3 fusion.147
  119.6 1.3 fusion.146
  120.9 1.2 convolution_multiply_fusion.3
  122.1 1.3 fusion.147
  124.1 1.3 fusion.146
  125.4 1.2 convolution_multiply_fusion.3
  126.6 1.3 fusion.147
  128.6 1.3 fusion.146
  131.0 2.2 %collective-permute-start.2 = (f32[131072]{0:T(1024)S(1)}, f32[131072]{0:T(1024)S(1)}, u32[]{:S(2)}, u32[]{:S(2)}) collective-permute-start(f32[131072]{0:T(1024)S(1)} %broadcast_select_fusion), channel_id=1, source_target_pairs={{0,1},{1,0},{2,3},{3,2},{4,5},{5,4},{6,7},{7,6},{8,9},{9,8},{10,11... | collective-permute-start | bytes 1572872 | tf_op jit(solution)/shard_map/ppermute | solution.py:38
  133.2 1.5 collective-permute-done.2
  134.9 2.2 %collective-permute-start.3 = (f32[65536]{0:T(1024)S(1)}, f32[65536]{0:T(1024)S(1)}, u32[]{:S(2)}, u32[]{:S(2)}) collective-permute-start(f32[65536]{0:T(1024)S(1)} %slice_select_fusion), channel_id=1, source_target_pairs={{0,2},{1,3},{2,0},{3,1},{4,6},{5,7},{6,4},{7,5},{8,10},{9,11},{10,... | collective-permute-start | bytes 786440 | tf_op jit(solution)/shard_map/ppermute | solution.py:38
  137.1 6.4 %collective-permute-done.3 = f32[65536]{0:T(1024)S(1)} collective-permute-done((f32[65536]{0:T(1024)S(1)}, f32[65536]{0:T(1024)S(1)}, u32[]{:S(2)}, u32[]{:S(2)}) %collective-permute-start.3) | collective-permute-done | bytes 262176 | tf_op jit(solution)/shard_map/ppermute | solution.py:38
  143.9 3.9 %collective-permute-done.4 = f32[32768]{0:T(1024)S(1)} collective-permute-done((f32[32768]{0:T(1024)S(1)}, f32[32768]{0:T(1024)S(1)}, u32[]{:S(2)}, u32[]{:S(2)}) %collective-permute-start.4) | collective-permute-done | bytes 131104 | tf_op jit(solution)/shard_map/ppermute | solution.py:38
  147.9 3.1 %collective-permute-done.5 = f32[16384]{0:T(1024)S(1)} collective-permute-done((f32[16384]{0:T(1024)S(1)}, f32[16384]{0:T(1024)S(1)}, u32[]{:S(2)}, u32[]{:S(2)}) %collective-permute-start.5) | collective-permute-done | bytes 65568 | tf_op jit(solution)/shard_map/ppermute | solution.py:38
  151.1 3.7 %collective-permute-done.6 = f32[8192]{0:T(1024)S(1)} collective-permute-done((f32[8192]{0:T(1024)S(1)}, f32[8192]{0:T(1024)S(1)}, u32[]{:S(2)}, u32[]{:S(2)}) %collective-permute-start.6) | collective-permute-done | bytes 32800 | tf_op jit(solution)/shard_map/ppermute | solution.py:38
  154.8 4.2 %collective-permute-done.7 = f32[8192]{0:T(1024)S(1)} collective-permute-done((f32[8192]{0:T(1024)S(1)}, f32[8192]{0:T(1024)S(1)}, u32[]{:S(2)}, u32[]{:S(2)}) %collective-permute-start.7) | collective-permute-done | bytes 32800 | tf_op jit(solution)/shard_map/ppermute | solution.py:42
  159.1 3.1 %collective-permute-done.8 = f32[16384]{0:T(1024)S(1)} collective-permute-done((f32[16384]{0:T(1024)S(1)}, f32[16384]{0:T(1024)S(1)}, u32[]{:S(2)}, u32[]{:S(2)}) %collective-permute-start.8) | collective-permute-done | bytes 65568 | tf_op jit(solution)/shard_map/ppermute | solution.py:42
  162.7 3.4 %collective-permute-done.9 = f32[32768]{0:T(1024)S(1)} collective-permute-done((f32[32768]{0:T(1024)S(1)}, f32[32768]{0:T(1024)S(1)}, u32[]{:S(2)}, u32[]{:S(2)}) %collective-permute-start.9) | collective-permute-done | bytes 131104 | tf_op jit(solution)/shard_map/ppermute | solution.py:42
  166.1 1.3 collective-permute-start.10
  167.5 7.8 %collective-permute-start.1 = (bf16[4,128,256]{2,1,0:T(8,128)(2,1)S(1)}, bf16[4,128,256]{2,1,0:T(8,128)(2,1)S(1)}, u32[]{:S(2)}, u32[]{:S(2)}) collective-permute-start(bf16[4,128,256]{2,1,0:T(8,128)(2,1)S(1)} %copy-done.13), channel_id=1, source_target_pairs={{0,7},{1,0},{2,1},{3,2},{4,3},{5,4},{6,5},{7,6},{8,15},{9,8},{10,9... | collective-permute-start | bytes 786440 | tf_op jit(solution)/shard_map/ppermute | solution.py:12
  175.3 4.9 %collective-permute-start.11 = (f32[131072]{0:T(1024)S(1)}, f32[131072]{0:T(1024)S(1)}, u32[]{:S(2)}, u32[]{:S(2)}) collective-permute-start(f32[131072]{0:T(1024)S(1)} %maximum_select_fusion.2), channel_id=1, source_target_pairs={{0,1},{1,0},{2,3},{3,2},{4,5},{5,4},{6,7},{7,6},{8,9},{9,8},{10,11... | collective-permute-start | bytes 1572872 | tf_op jit(solution)/shard_map/ppermute | solution.py:42
  180.2 2.0 %collective-permute-done.1 = bf16[4,128,256]{2,1,0:T(8,128)(2,1)S(1)} collective-permute-done((bf16[4,128,256]{2,1,0:T(8,128)(2,1)S(1)}, bf16[4,128,256]{2,1,0:T(8,128)(2,1)S(1)}, u32[]{:S(2)}, u32[]{:S(2)}) %collective-permute-start.1) | collective-permute-done | bytes 262176 | tf_op jit(solution)/shard_map/ppermute | solution.py:12
  182.2 1.5 convolution_add_fusion.4
  (149 shorter events, 32.9 us)
Async XLA Ops:
  0.6 50.3 %copy-start = (bf16[256,256]{1,0:T(8,128)(2,1)S(1)}, bf16[256,256]{1,0:T(8,128)(2,1)}, u32[]{:S(2)}) copy-start(bf16[256,256]{1,0:T(8,128)(2,1)} %param.20) | copy-start | bytes 393220
  2.1 13.3 %copy-start.1 = (bf16[4,256,256]{2,1,0:T(8,128)(2,1)S(1)}, bf16[4,256,256]{2,1,0:T(8,128)(2,1)}, u32[]{:S(2)}) copy-start(bf16[4,256,256]{2,1,0:T(8,128)(2,1)} %param.14) | copy-start | bytes 1572868
  2.1 13.3 %copy-start.2 = (bf16[256,256]{1,0:T(8,128)(2,1)S(1)}, bf16[256,256]{1,0:T(8,128)(2,1)}, u32[]{:S(2)}) copy-start(bf16[256,256]{1,0:T(8,128)(2,1)} %param.19) | copy-start | bytes 393220
  9.4 6.0 %collective-permute-start = (bf16[4,128,256]{2,1,0:T(8,128)(2,1)S(1)}, bf16[4,128,256]{2,1,0:T(8,128)(2,1)S(1)}, u32[]{:S(2)}, u32[]{:S(2)}) collective-permute-start(bf16[4,128,256]{2,1,0:T(8,128)(2,1)S(1)} %select_select_fusion), channel_id=1, source_target_pairs={{0,1},{1,2},{2,3},{3,4},{4,5},{5,6},{6,7},{7,0},{8,9},{9,10},{10,1... | collective-permute-start | bytes 786440 | tf_op jit(solution)/shard_map/ppermute | solution.py:12
  30.2 5.8 %copy-start.7 = (f32[4,256,256]{2,1,0:T(8,128)}, f32[4,256,256]{2,1,0:T(8,128)S(1)}, u32[]{:S(2)}) copy-start(f32[4,256,256]{2,1,0:T(8,128)S(1)} %get-tuple-element.424) | copy-start | bytes 3145732
  30.2 5.8 %copy-start.3 = (bf16[16,1,1,64,256]{4,3,2,1,0:T(8,128)(2,1)S(1)}, bf16[16,1,1,64,256]{4,3,2,1,0:T(8,128)(2,1)}, u32[]{:S(2)}) copy-start(bf16[16,1,1,64,256]{4,3,2,1,0:T(8,128)(2,1)} %param.23) | copy-start | bytes 1572868
  31.4 17.7 %all-to-all-start = ((bf16[4,256,256]{2,0,1:T(4,128)(2,1)}), bf16[4,256,256]{2,0,1:T(4,128)(2,1)S(1)}, u32[]{:S(2)}, u32[]{:S(2)}) async-start(bf16[4,256,256]{2,0,1:T(4,128)(2,1)} %copy.52), calls=%async_computation | async-start | bytes 1048576 | tf_op jit(solution)/shard_map/all_to_all | solution.py:185
  36.0 13.2 %copy-start.10 = (bf16[256,256]{1,0:T(8,128)(2,1)S(1)}, bf16[256,256]{1,0:T(8,128)(2,1)}, u32[]{:S(2)}) copy-start(bf16[256,256]{1,0:T(8,128)(2,1)} %param.21) | copy-start | bytes 393220
  49.5 3.1 %copy-start.9 = (bf16[256,256]{1,0:T(8,128)(2,1)S(1)}, bf16[256,256]{1,0:T(8,128)(2,1)}, u32[]{:S(2)}) copy-start(bf16[256,256]{1,0:T(8,128)(2,1)} %param.22) | copy-start | bytes 393220
  63.9 6.2 %copy-start.6 = (bf16[16,64,4,64]{3,2,1,0:T(4,128)(2,1)S(1)}, bf16[16,64,4,64]{3,2,1,0:T(4,128)(2,1)}, u32[]{:S(2)}) copy-start(bf16[16,64,4,64]{3,2,1,0:T(4,128)(2,1)} %reshape.172) | copy-start | bytes 1572868
  87.9 1.4 copy-start.11
  93.3 5.0 %copy-start.4 = (f32[32,2,8,128]{3,2,1,0:T(8,128)S(1)}, f32[32,2,8,128]{3,2,1,0:T(8,128)}, u32[]{:S(2)}) copy-start(f32[32,2,8,128]{3,2,1,0:T(8,128)} %convolution_bitcast_fusion.3) | copy-start | bytes 786436
  93.7 5.5 %copy-start.5 = (f32[32,2,8,128]{3,2,1,0:T(8,128)S(1)}, f32[32,2,8,128]{3,2,1,0:T(8,128)}, u32[]{:S(2)}) copy-start(f32[32,2,8,128]{3,2,1,0:T(8,128)} %convolution_bitcast_fusion.2) | copy-start | bytes 786436
  94.9 16.7 %all-to-all-start.1 = ((bf16[16,64,256]{2,1,0:T(8,128)(2,1)}), bf16[16,64,256]{2,1,0:T(8,128)(2,1)S(1)}, u32[]{:S(2)}, u32[]{:S(2)}) async-start(bf16[16,64,256]{2,1,0:T(8,128)(2,1)} %bitcast.30), calls=%async_computation.1 | async-start | bytes 1048576 | tf_op jit(solution)/shard_map/all_to_all | solution.py:188
  129.9 1.0 copy-start.8
  131.0 3.8 %collective-permute-start.2 = (f32[131072]{0:T(1024)S(1)}, f32[131072]{0:T(1024)S(1)}, u32[]{:S(2)}, u32[]{:S(2)}) collective-permute-start(f32[131072]{0:T(1024)S(1)} %broadcast_select_fusion), channel_id=1, source_target_pairs={{0,1},{1,0},{2,3},{3,2},{4,5},{5,4},{6,7},{7,6},{8,9},{9,8},{10,11... | collective-permute-start | bytes 1572872 | tf_op jit(solution)/shard_map/ppermute | solution.py:38
  134.9 32.6 %copy-start.13 = (bf16[4,128,256]{2,1,0:T(8,128)(2,1)S(1)}, bf16[4,128,256]{2,1,0:T(8,128)(2,1)}, u32[]{:S(2)}) copy-start(bf16[4,128,256]{2,1,0:T(8,128)(2,1)} %get-tuple-element.126) | copy-start | bytes 786436
  134.9 8.6 %collective-permute-start.3 = (f32[65536]{0:T(1024)S(1)}, f32[65536]{0:T(1024)S(1)}, u32[]{:S(2)}, u32[]{:S(2)}) collective-permute-start(f32[65536]{0:T(1024)S(1)} %slice_select_fusion), channel_id=1, source_target_pairs={{0,2},{1,3},{2,0},{3,1},{4,6},{5,7},{6,4},{7,5},{8,10},{9,11},{10,... | collective-permute-start | bytes 786440 | tf_op jit(solution)/shard_map/ppermute | solution.py:38
  137.1 45.1 %copy-start.12 = (s32[4,128]{1,0:T(4,128)S(1)}, s32[4,128]{1,0:T(4,128)}, u32[]{:S(2)}) copy-start(s32[4,128]{1,0:T(4,128)} %param.17) | copy-start | bytes 6148
  143.6 4.2 %collective-permute-start.4 = (f32[32768]{0:T(1024)S(1)}, f32[32768]{0:T(1024)S(1)}, u32[]{:S(2)}, u32[]{:S(2)}) collective-permute-start(f32[32768]{0:T(1024)S(1)} %slice_select_fusion.1), channel_id=1, source_target_pairs={{0,4},{1,5},{2,6},{3,7},{4,0},{5,1},{6,2},{7,3},{8,12},{9,13},{10,... | collective-permute-start | bytes 393224 | tf_op jit(solution)/shard_map/ppermute | solution.py:38
  147.8 3.2 %collective-permute-start.5 = (f32[16384]{0:T(1024)S(1)}, f32[16384]{0:T(1024)S(1)}, u32[]{:S(2)}, u32[]{:S(2)}) collective-permute-start(f32[16384]{0:T(1024)S(1)} %slice_select_fusion.2), channel_id=1, source_target_pairs={{0,8},{8,0},{16,24},{24,16},{1,9},{9,1},{17,25},{25,17},{2,10},{10... | collective-permute-start | bytes 196616 | tf_op jit(solution)/shard_map/ppermute | solution.py:38
  151.0 3.8 %collective-permute-start.6 = (f32[8192]{0:T(1024)S(1)}, f32[8192]{0:T(1024)S(1)}, u32[]{:S(2)}, u32[]{:S(2)}) collective-permute-start(f32[8192]{0:T(1024)S(1)} %slice_select_fusion.3), channel_id=1, source_target_pairs={{0,16},{8,24},{16,0},{24,8},{1,17},{9,25},{17,1},{25,9},{2,18},{10... | collective-permute-start | bytes 98312 | tf_op jit(solution)/shard_map/ppermute | solution.py:38
  154.8 4.2 %collective-permute-start.7 = (f32[8192]{0:T(1024)S(1)}, f32[8192]{0:T(1024)S(1)}, u32[]{:S(2)}, u32[]{:S(2)}) collective-permute-start(f32[8192]{0:T(1024)S(1)} %select_add_fusion.4), channel_id=1, source_target_pairs={{0,16},{8,24},{16,0},{24,8},{1,17},{9,25},{17,1},{25,9},{2,18},{10... | collective-permute-start | bytes 98312 | tf_op jit(solution)/shard_map/ppermute | solution.py:42
  159.0 3.2 %collective-permute-start.8 = (f32[16384]{0:T(1024)S(1)}, f32[16384]{0:T(1024)S(1)}, u32[]{:S(2)}, u32[]{:S(2)}) collective-permute-start(f32[16384]{0:T(1024)S(1)} %maximum_select_fusion.7), channel_id=1, source_target_pairs={{0,8},{8,0},{16,24},{24,16},{1,9},{9,1},{17,25},{25,17},{2,10},{10... | collective-permute-start | bytes 196616 | tf_op jit(solution)/shard_map/ppermute | solution.py:42
  162.2 3.9 %collective-permute-start.9 = (f32[32768]{0:T(1024)S(1)}, f32[32768]{0:T(1024)S(1)}, u32[]{:S(2)}, u32[]{:S(2)}) collective-permute-start(f32[32768]{0:T(1024)S(1)} %maximum_select_fusion.6), channel_id=1, source_target_pairs={{0,4},{1,5},{2,6},{3,7},{4,0},{5,1},{6,2},{7,3},{8,12},{9,13},{10,... | collective-permute-start | bytes 393224 | tf_op jit(solution)/shard_map/ppermute | solution.py:42
  166.1 9.2 %collective-permute-start.10 = (f32[65536]{0:T(1024)S(1)}, f32[65536]{0:T(1024)S(1)}, u32[]{:S(2)}, u32[]{:S(2)}) collective-permute-start(f32[65536]{0:T(1024)S(1)} %maximum_select_fusion.4), channel_id=1, source_target_pairs={{0,2},{1,3},{2,0},{3,1},{4,6},{5,7},{6,4},{7,5},{8,10},{9,11},{10,... | collective-permute-start | bytes 786440 | tf_op jit(solution)/shard_map/ppermute | solution.py:42
  167.5 14.7 %collective-permute-start.1 = (bf16[4,128,256]{2,1,0:T(8,128)(2,1)S(1)}, bf16[4,128,256]{2,1,0:T(8,128)(2,1)S(1)}, u32[]{:S(2)}, u32[]{:S(2)}) collective-permute-start(bf16[4,128,256]{2,1,0:T(8,128)(2,1)S(1)} %copy-done.13), channel_id=1, source_target_pairs={{0,7},{1,0},{2,1},{3,2},{4,3},{5,4},{6,5},{7,6},{8,15},{9,8},{10,9... | collective-permute-start | bytes 786440 | tf_op jit(solution)/shard_map/ppermute | solution.py:12
  175.3 8.6 %collective-permute-start.11 = (f32[131072]{0:T(1024)S(1)}, f32[131072]{0:T(1024)S(1)}, u32[]{:S(2)}, u32[]{:S(2)}) collective-permute-start(f32[131072]{0:T(1024)S(1)} %maximum_select_fusion.2), channel_id=1, source_target_pairs={{0,1},{1,0},{2,3},{3,2},{4,5},{5,4},{6,7},{7,6},{8,9},{9,8},{10,11... | collective-permute-start | bytes 1572872 | tf_op jit(solution)/shard_map/ppermute | solution.py:42
where the time goes:
time: 186 us; the launch traced here: 185 us
  waiting for transfers between devices  59.3 us (32%)
  matrix products  54.4 us (29%)
  local copies, waits for them, and re-layouts  36.9 us (20%)
  starting transfers between devices  30.2 us (16%)
  other arithmetic  2.89 us (2%)
    ppermute x5, waiting for transfers between devices, tree_sum(): flat = keep + lax.ppermute(send, axis, pairs)  18.6 us
    all_to_all x1, waiting for transfers between devices, local(): lax.all_to_all(hidden, 'day', split_axis=1, concat_axis=0, tiled=True)  12.6 us
    all_to_all x1, waiting for transfers between devices, local(): lax.all_to_all(back, 'day', split_axis=0, concat_axis=1, tiled=True)  12 us
    ppermute x5, waiting for transfers between devices, tree_sum(): other = lax.ppermute(flat, axis, pairs)  10.7 us
    ppermute x2, starting transfers between devices, from_behind(): return lax.ppermute(value, axis, pairs)  10.5 us
    gather x1, local copies, waits for them, and re-layouts, local(): picked = jnp.take_along_axis(node_states, halo_rows[:, :, None], axis=1)  7 us
    ppermute x5, starting transfers between devices, tree_sum(): other = lax.ppermute(flat, axis, pairs)  6.72 us
    dot_general x1, matrix products, attend(): jnp.einsum('nhts,tnhd->snhd', score_f, query_f).astype(jnp.bfloat16)  6.16 us
  transfers between devices with their start and end apart: 14, of which 12 were waited for; matrix products, arithmetic and copies ran while one was open for 2% of the time, Pallas kernels for 0%

commit v1 on v0

--- a/solution.py
+++ b/solution.py
@@ -4,6 +4,23 @@
 from jax.sharding import PartitionSpec as P
 
 HEADS = 4
+
+
+def run_terms(vec, row_dim, obj):
+    tall = vec.shape
+    return jnp.moveaxis(
+        vec.reshape(*tall[:row_dim], obj, tall[row_dim] // obj, *tall[row_dim + 1 :]), row_dim, 0
+    )
+
+
+def define_limits(local_block, along_dim):
+    local_block = jnp.moveaxis(local_block, 0, along_dim)
+    response = local_block.shape
+    return local_block.reshape(
+        *response[:along_dim],
+        response[along_dim] * response[along_dim + 1],
+        *response[along_dim + 2 :]
+    )
 
 
 def from_behind(value, axis, steps):
@@ -182,7 +199,21 @@
     aggregate, preact, inverse, hidden, adjacent = lax.map(
         forward_one, (node_states, received, edge_source, edge_target)
     )
-    node_major = lax.all_to_all(hidden, "day", split_axis=1, concat_axis=0, tiled=True)
+    all_rows = jax.lax.axis_size("day")
+    shaped, taken_in = (all_rows, jax.lax.axis_index("day"))
+    all_values = run_terms(hidden, 1, shaped)
+    dev_i = 1
+    ledger = [all_values[taken_in]]
+    while dev_i < shaped:
+        block_last = all_values[(taken_in + dev_i) % shaped]
+        ledger.append(
+            jax.lax.ppermute(
+                block_last, "day", [(it, (it + dev_i) % shaped) for it in range(shaped)]
+            )
+        )
+        dev_i += 1
+    all_values = jnp.stack(ledger, axis=0)[(taken_in - jnp.arange(shaped)) % shaped]
+    node_major = define_limits(all_values, 0)
     upstream = cotangent.reshape(cotangent.shape[0], -1, width)
     attn_grads, back = attend(node_major, upstream, w_query, w_key, w_value)
     back_days = lax.all_to_all(back, "day", split_axis=0, concat_axis=1, tiled=True)

time: 186 us -> 176 us (0.946)
  waiting for transfers between devices: 59.3 us -> 52.4 us
  matrix products: 54.4 us -> 51.6 us
  local copies, waits for them, and re-layouts: 36.9 us -> 34.5 us
  starting transfers between devices: 30.2 us -> 32.5 us
    all_to_all x1 -> x0, waiting for transfers between devices: 12.6 us -> none  [local(): lax.all_to_all(hidden, 'day', split_axis=1, concat_axis=0, tiled=True)]
    ppermute x0 -> x3, waiting for transfers between devices: none -> 7.79 us  [local(): jax.lax.ppermute(block_last, 'day', [(it, (it + dev_i) % shaped) for it i...]
    ppermute x0 -> x3, starting transfers between devices: none -> 4.72 us  [local(): jax.lax.ppermute(block_last, 'day', [(it, (it + dev_i) % shaped) for it i...]
    all_to_all x1 -> x0, starting transfers between devices: 4.59 us -> none  [local(): lax.all_to_all(hidden, 'day', split_axis=1, concat_axis=0, tiled=True)]
    ppermute x5, waiting for transfers between devices: 18.6 us -> 16.7 us  [tree_sum(): flat = keep + lax.ppermute(send, axis, pairs)]
  transfers between devices with their start and end apart: 14 -> 16, of which waited for: 12 -> 13; matrix products, arithmetic and copies ran while one was open for 2% -> 2% of each run, Pallas kernels for 0% -> 0%
where the time goes in v1:
time: 176 us; the launch traced here: 175 us
  waiting for transfers between devices  52.4 us (30%)
  matrix products  51.6 us (29%)
  local copies, waits for them, and re-layouts  34.5 us (20%)
  starting transfers between devices  32.5 us (18%)
  other arithmetic  2.97 us (2%)
    ppermute x5, waiting for transfers between devices, tree_sum(): flat = keep + lax.ppermute(send, axis, pairs)  16.7 us
    all_to_all x1, waiting for transfers between devices, local(): lax.all_to_all(back, 'day', split_axis=0, concat_axis=1, tiled=True)  12.8 us
    ppermute x2, starting transfers between devices, from_behind(): return lax.ppermute(value, axis, pairs)  10.5 us
    ppermute x5, waiting for transfers between devices, tree_sum(): other = lax.ppermute(flat, axis, pairs)  9.8 us
    ppermute x5, starting transfers between devices, tree_sum(): other = lax.ppermute(flat, axis, pairs)  8.13 us
    ppermute x3, waiting for transfers between devices, local(): jax.lax.ppermute(block_last, 'day', [(it, (it + dev_i) % shaped) for it i...  7.79 us
    gather x1, local copies, waits for them, and re-layouts, local(): picked = jnp.take_along_axis(node_states, halo_rows[:, :, None], axis=1)  7 us
    dot_general x1, matrix products, attend(): jnp.einsum('nhts,tnhd->snhd', score_f, query_f).astype(jnp.bfloat16)  6.13 us
  transfers between devices with their start and end apart: 16, of which 13 were waited for; matrix products, arithmetic and copies ran while one was open for 2% of the time, Pallas kernels for 0%

profile of v1, /device:TPU:1, one launch (start us, length us, event | category | flops | bytes accessed | tf_op | source)
XLA Modules:
  0.0 175.5 jit_solution(10363302863783780085)
XLA Ops:
  2.1 7.0 %gather_fusion.1 = bf16[512,256]{1,0:T(8,128)(2,1)S(1)} fusion(bf16[4,256,256]{2,1,0:T(8,128)(2,1)} %param.14, s32[512]{0:T(512)S(1)} %fusion.70), kind=kCustom, calls=%fused_computation.1 | custom fusion | bytes 528384 | tf_op jit(solution)/shard_map/jit(take_along_axis)/gather | solution.py:190
  9.4 2.7 %collective-permute-start = (bf16[4,128,256]{2,1,0:T(8,128)(2,1)S(1)}, bf16[4,128,256]{2,1,0:T(8,128)(2,1)S(1)}, u32[]{:S(2)}, u32[]{:S(2)}) collective-permute-start(bf16[4,128,256]{2,1,0:T(8,128)(2,1)S(1)} %select_select_fusion), channel_id=1, source_target_pairs={{0,1},{1,2},{2,3},{3,4},{4,5},{5,6},{6,7},{7,0},{8,9},{9,10},{10,1... | collective-permute-start | bytes 786440 | tf_op jit(solution)/shard_map/ppermute | solution.py:29
  12.0 3.3 %collective-permute-done = bf16[4,128,256]{2,1,0:T(8,128)(2,1)S(1)} collective-permute-done((bf16[4,128,256]{2,1,0:T(8,128)(2,1)S(1)}, bf16[4,128,256]{2,1,0:T(8,128)(2,1)S(1)}, u32[]{:S(2)}, u32[]{:S(2)}) %collective-permute-start) | collective-permute-done | bytes 262176 | tf_op jit(solution)/shard_map/ppermute | solution.py:29
  15.4 14.8 %while.34 = (s32[]{:T(128)}, bf16[4,256,256]{2,1,0:T(8,128)(2,1)}, f32[4,256,256]{2,1,0:T(8,128)S(1)}, f32[4,256]{1,0:T(4,128)S(1)}, bf16[4,256,256]{2,1,0:T(8,1...) while((s32[]{:T(128)}, bf16[4,256,256]{2,1,0:T(8,128)(2,1)}, ...), condition=%wide.region_2.3_spmd.clone, body=%wide.region_0.2_spmd.sunk.clone | while | flops 287277312 | bytes 3112069 | solution.py:199
  30.3 1.3 collective-permute-start.1
  31.7 2.3 %collective-permute-start.2 = (bf16[4,64,256]{2,1,0:T(8,128)(2,1)S(1)}, bf16[4,64,256]{2,1,0:T(8,128)(2,1)S(1)}, u32[]{:S(2)}, u32[]{:S(2)}) collective-permute-start(bf16[4,64,256]{2,1,0:T(8,128)(2,1)S(1)} %get-tuple-element.184), channel_id=1, source_target_pairs={{0,16},{8,24},{16,0},{24,8},{1,17},{9,25},{17,1},{25,9},{2,18},{10... | collective-permute-start | bytes 393224 | tf_op jit(solution)/shard_map/ppermute | solution.py:210
  36.2 7.2 %collective-permute-done.2 = bf16[4,64,256]{2,1,0:T(8,128)(2,1)S(1)} collective-permute-done((bf16[4,64,256]{2,1,0:T(8,128)(2,1)S(1)}, bf16[4,64,256]{2,1,0:T(8,128)(2,1)S(1)}, u32[]{:S(2)}, u32[]{:S(2)}) %collective-permute-start.2) | collective-permute-done | bytes 131104 | tf_op jit(solution)/shard_map/ppermute | solution.py:210
  44.3 1.4 reshape.227
  46.0 1.5 reshape.228
  48.2 2.6 %fusion.52 = f32[64,4,16,16]{3,2,1,0:T(8,128)} fusion(bf16[16,64,4,64]{3,2,1,0:T(4,128)(2,1)S(1)} %reshape.229, bf16[16,64,4,64]{3,2,1,0:T(4,128)(2,1)S(1)} %reshape_reshape.8), kind=kOutput, calls=%fused_computation.92 | convolution fusion | flops 8388608 | bytes 1310720 | tf_op jit(solution)/shard_map/tnhd,snhd->nhts/dot_general | solution.py:143
  50.8 4.9 %fusion.80 = (f32[64,4,16]{2,1,0:T(4,128)S(1)}, f32[64,4,16,16]{2,3,1,0:T(8,128)}) fusion(pred[16,16]{0,1:T(8,128)(4,1)S(1)} %iota_compare_fusion.7, bf16[16,64,4,64]{3,2,1,0:T(4,128)(2,1)} %reshape.227, bf16[16,64,4,64]{3,2,1,0:T(4,128)(2,1)} %reshape.228), kind=kOutput, calls=%fused_computation.158 | convolution fusion | flops 8650767 | bytes 1327360 | tf_op jit(solution)/shard_map/sub | solution.py:138
  55.7 3.5 %fusion.49 = bf16[16,64,4,64]{3,0,2,1:T(8,128)(2,1)} fusion(bf16[16,64,4,64]{3,2,1,0:T(4,128)(2,1)S(1)} %reshape_reshape.8, f32[64,4,16,16]{2,3,1,0:T(8,128)} %get-tuple-element.187, f32[64,4,16]{2,1,0:T(4,128)S(1)} %get-tuple-element.186), kind=kOutput, calls=%fused_computation.78 | convolution fusion | flops 8781824 | bytes 1327104 | tf_op jit(solution)/shard_map/nhts,tnhd->snhd/dot_general | solution.py:142
  59.1 6.1 %fusion.50 = bf16[16,64,4,64]{3,0,2,1:T(8,128)(2,1)} fusion(f32[64,4,16,16]{3,2,1,0:T(8,128)} %fusion.52, bf16[16,64,4,64]{3,2,1,0:T(4,128)(2,1)} %reshape.228, f32[64,4,16,16]{2,3,1,0:T(8,128)} %get-tuple-element.187, f32[64,4,16]{2,1,0:T(4,128)S(1)} %get-tuple-element.186), kind=kOutput, calls=%fused_computation.79 | convolution fusion | flops 9113615 | bytes 1589248 | tf_op jit(solution)/shard_map/nhts,tnhd->snhd/dot_general | solution.py:149
  65.3 4.9 %fusion.48 = bf16[16,64,4,64]{3,0,2,1:T(8,128)(2,1)} fusion(f32[64,4,16,16]{3,2,1,0:T(8,128)S(1)} %copy-done.4, bf16[16,64,4,64]{3,2,1,0:T(4,128)(2,1)} %reshape.227, f32[64,4,16,16]{2,3,1,0:T(8,128)} %get-tuple-element.187, f32[64,4,16]{2,1,0:T(4,128)S(1)} %get-tuple-element.186), kind=kOutput, calls=%fused_computation.77 | convolution fusion | flops 9113615 | bytes 1589248 | tf_op jit(solution)/shard_map/nhts,snhd->tnhd/dot_general | solution.py:148
  70.2 2.9 %copy.35 = bf16[16,64,4,64]{1,0,3,2:T(8,128)(2,1)S(1)} copy(bf16[16,64,4,64]{3,0,2,1:T(8,128)(2,1)} %fusion.49) | data formatting | bytes 1048576 | tf_op jit(solution)/shard_map/convert_element_type | solution.py:142
  73.8 2.9 %copy.33 = bf16[16,64,4,64]{1,0,3,2:T(8,128)(2,1)S(1)} copy(bf16[16,64,4,64]{3,0,2,1:T(8,128)(2,1)} %fusion.50) | data formatting | bytes 1048576 | tf_op jit(solution)/shard_map/convert_element_type | solution.py:149
  77.4 2.9 %copy.31 = bf16[16,64,4,64]{1,0,3,2:T(8,128)(2,1)S(1)} copy(bf16[16,64,4,64]{3,0,2,1:T(8,128)(2,1)} %fusion.48) | data formatting | bytes 1048576 | tf_op jit(solution)/shard_map/convert_element_type | solution.py:148
  81.4 1.4 convolution_add_fusion.3
  85.1 4.3 %all-to-all-start = ((bf16[16,64,256]{2,1,0:T(8,128)(2,1)}), bf16[16,64,256]{2,1,0:T(8,128)(2,1)S(1)}, u32[]{:S(2)}, u32[]{:S(2)}) async-start(bf16[16,64,256]{2,1,0:T(8,128)(2,1)} %bitcast.37), calls=%async_computation | async-start | bytes 1048576 | tf_op jit(solution)/shard_map/all_to_all | solution.py:219
  90.6 12.8 %all-to-all-done = bf16[16,64,256]{2,1,0:T(8,128)(2,1)S(1)} async-done(((bf16[16,64,256]{2,1,0:T(8,128)(2,1)}), bf16[16,64,256]{2,1,0:T(8,128)(2,1)S(1)}, u32[]{:S(2)}, u32[]{:S(2)}) %all-to-all-start) | async-done | bytes 524320 | tf_op jit(solution)/shard_map/all_to_all | solution.py:219
  103.6 18.2 %while.35 = (s32[]{:T(128)}, f32[4,256,256]{2,1,0:T(8,128)S(1)}, f32[4,256,256]{2,1,0:T(8,128)S(1)}, bf16[4,128,256]{2,1,0:T(8,128)(2,1)}, bf16[4,256,256]{2,1,0...) while((s32[]{:T(128)}, f32[4,256,256]{2,1,0:T(8,128)S(1)}, ...), condition=%wide.region_7.8_spmd.clone, body=%wide.region_6.7_spmd.sunk.clone | while | flops 370671616 | bytes 3479661 | solution.py:224
  103.7 1.2 convolution_multiply_fusion.3
  104.9 1.3 fusion.149
  106.9 1.3 fusion.148
  108.2 1.2 convolution_multiply_fusion.3
  109.4 1.3 fusion.149
  111.4 1.3 fusion.148
  112.7 1.2 convolution_multiply_fusion.3
  114.0 1.3 fusion.149
  116.0 1.3 fusion.148
  117.3 1.2 convolution_multiply_fusion.3
  118.5 1.3 fusion.149
  120.5 1.3 fusion.148
  122.8 1.5 collective-permute-start.5
  124.4 1.5 collective-permute-done.5
  126.0 1.2 collective-permute-start.6
  127.3 6.3 %collective-permute-done.6 = f32[65536]{0:T(1024)S(1)} collective-permute-done((f32[65536]{0:T(1024)S(1)}, f32[65536]{0:T(1024)S(1)}, u32[]{:S(2)}, u32[]{:S(2)}) %collective-permute-start.6) | collective-permute-done | bytes 262176 | tf_op jit(solution)/shard_map/ppermute | solution.py:55
  134.9 2.7 %collective-permute-done.7 = f32[32768]{0:T(1024)S(1)} collective-permute-done((f32[32768]{0:T(1024)S(1)}, f32[32768]{0:T(1024)S(1)}, u32[]{:S(2)}, u32[]{:S(2)}) %collective-permute-start.7) | collective-permute-done | bytes 131104 | tf_op jit(solution)/shard_map/ppermute | solution.py:55
  137.7 3.1 %collective-permute-done.8 = f32[16384]{0:T(1024)S(1)} collective-permute-done((f32[16384]{0:T(1024)S(1)}, f32[16384]{0:T(1024)S(1)}, u32[]{:S(2)}, u32[]{:S(2)}) %collective-permute-start.8) | collective-permute-done | bytes 65568 | tf_op jit(solution)/shard_map/ppermute | solution.py:55
  141.6 3.0 %collective-permute-done.9 = f32[8192]{0:T(1024)S(1)} collective-permute-done((f32[8192]{0:T(1024)S(1)}, f32[8192]{0:T(1024)S(1)}, u32[]{:S(2)}, u32[]{:S(2)}) %collective-permute-start.9) | collective-permute-done | bytes 32800 | tf_op jit(solution)/shard_map/ppermute | solution.py:55
  145.3 4.0 %collective-permute-done.10 = f32[8192]{0:T(1024)S(1)} collective-permute-done((f32[8192]{0:T(1024)S(1)}, f32[8192]{0:T(1024)S(1)}, u32[]{:S(2)}, u32[]{:S(2)}) %collective-permute-start.10) | collective-permute-done | bytes 32800 | tf_op jit(solution)/shard_map/ppermute | solution.py:59
  149.4 3.1 %collective-permute-done.11 = f32[16384]{0:T(1024)S(1)} collective-permute-done((f32[16384]{0:T(1024)S(1)}, f32[16384]{0:T(1024)S(1)}, u32[]{:S(2)}, u32[]{:S(2)}) %collective-permute-start.11) | collective-permute-done | bytes 65568 | tf_op jit(solution)/shard_map/ppermute | solution.py:59
  153.7 2.7 %collective-permute-done.12 = f32[32768]{0:T(1024)S(1)} collective-permute-done((f32[32768]{0:T(1024)S(1)}, f32[32768]{0:T(1024)S(1)}, u32[]{:S(2)}, u32[]{:S(2)}) %collective-permute-start.12) | collective-permute-done | bytes 131104 | tf_op jit(solution)/shard_map/ppermute | solution.py:59
  156.4 1.2 collective-permute-start.13
  157.6 7.8 %collective-permute-start.4 = (bf16[4,128,256]{2,1,0:T(8,128)(2,1)S(1)}, bf16[4,128,256]{2,1,0:T(8,128)(2,1)S(1)}, u32[]{:S(2)}, u32[]{:S(2)}) collective-permute-start(bf16[4,128,256]{2,1,0:T(8,128)(2,1)S(1)} %copy-done.11), channel_id=1, source_target_pairs={{0,7},{1,0},{2,1},{3,2},{4,3},{5,4},{6,5},{7,6},{8,15},{9,8},{10,9... | collective-permute-start | bytes 786440 | tf_op jit(solution)/shard_map/ppermute | solution.py:29
  165.5 5.0 %collective-permute-start.14 = (f32[131072]{0:T(1024)S(1)}, f32[131072]{0:T(1024)S(1)}, u32[]{:S(2)}, u32[]{:S(2)}) collective-permute-start(f32[131072]{0:T(1024)S(1)} %maximum_select_fusion.2), channel_id=1, source_target_pairs={{0,1},{1,0},{2,3},{3,2},{4,5},{5,4},{6,7},{7,6},{8,9},{9,8},{10,11... | collective-permute-start | bytes 1572872 | tf_op jit(solution)/shard_map/ppermute | solution.py:59
  170.5 2.0 %collective-permute-done.4 = bf16[4,128,256]{2,1,0:T(8,128)(2,1)S(1)} collective-permute-done((bf16[4,128,256]{2,1,0:T(8,128)(2,1)S(1)}, bf16[4,128,256]{2,1,0:T(8,128)(2,1)S(1)}, u32[]{:S(2)}, u32[]{:S(2)}) %collective-permute-start.4) | collective-permute-done | bytes 262176 | tf_op jit(solution)/shard_map/ppermute | solution.py:29
  172.5 1.5 convolution_add_fusion.4
  (151 shorter events, 36.1 us)
Async XLA Ops:
  0.6 45.1 %copy-start = (bf16[256,256]{1,0:T(8,128)(2,1)S(1)}, bf16[256,256]{1,0:T(8,128)(2,1)}, u32[]{:S(2)}) copy-start(bf16[256,256]{1,0:T(8,128)(2,1)} %param.20) | copy-start | bytes 393220
  2.1 13.3 %copy-start.1 = (bf16[4,256,256]{2,1,0:T(8,128)(2,1)S(1)}, bf16[4,256,256]{2,1,0:T(8,128)(2,1)}, u32[]{:S(2)}) copy-start(bf16[4,256,256]{2,1,0:T(8,128)(2,1)} %param.14) | copy-start | bytes 1572868
  2.1 13.3 %copy-start.2 = (bf16[256,256]{1,0:T(8,128)(2,1)S(1)}, bf16[256,256]{1,0:T(8,128)(2,1)}, u32[]{:S(2)}) copy-start(bf16[256,256]{1,0:T(8,128)(2,1)} %param.19) | copy-start | bytes 393220
  9.4 6.0 %collective-permute-start = (bf16[4,128,256]{2,1,0:T(8,128)(2,1)S(1)}, bf16[4,128,256]{2,1,0:T(8,128)(2,1)S(1)}, u32[]{:S(2)}, u32[]{:S(2)}) collective-permute-start(bf16[4,128,256]{2,1,0:T(8,128)(2,1)S(1)} %select_select_fusion), channel_id=1, source_target_pairs={{0,1},{1,2},{2,3},{3,4},{4,5},{5,6},{6,7},{7,0},{8,9},{9,10},{10,1... | collective-permute-start | bytes 786440 | tf_op jit(solution)/shard_map/ppermute | solution.py:29
  15.4 19.7 %copy-start.3 = (bf16[16,1,1,64,256]{4,3,2,1,0:T(8,128)(2,1)S(1)}, bf16[16,1,1,64,256]{4,3,2,1,0:T(8,128)(2,1)}, u32[]{:S(2)}) copy-start(bf16[16,1,1,64,256]{4,3,2,1,0:T(8,128)(2,1)} %param.23) | copy-start | bytes 1572868
  30.3 4.8 %copy-start.5 = (f32[4,256,256]{2,1,0:T(8,128)}, f32[4,256,256]{2,1,0:T(8,128)S(1)}, u32[]{:S(2)}) copy-start(f32[4,256,256]{2,1,0:T(8,128)S(1)} %get-tuple-element.428) | copy-start | bytes 3145732
  30.3 13.7 %copy-start.8 = (bf16[256,256]{1,0:T(8,128)(2,1)S(1)}, bf16[256,256]{1,0:T(8,128)(2,1)}, u32[]{:S(2)}) copy-start(bf16[256,256]{1,0:T(8,128)(2,1)} %param.21) | copy-start | bytes 393220
  30.3 5.8 %collective-permute-start.1 = (bf16[4,64,256]{2,1,0:T(8,128)(2,1)S(1)}, bf16[4,64,256]{2,1,0:T(8,128)(2,1)S(1)}, u32[]{:S(2)}, u32[]{:S(2)}) collective-permute-start(bf16[4,64,256]{2,1,0:T(8,128)(2,1)S(1)} %get-tuple-element.185), channel_id=1, source_target_pairs={{0,8},{8,16},{16,24},{24,0},{1,9},{9,17},{17,25},{25,1},{2,10},{10... | collective-permute-start | bytes 393224 | tf_op jit(solution)/shard_map/ppermute | solution.py:210
  31.7 11.7 %collective-permute-start.2 = (bf16[4,64,256]{2,1,0:T(8,128)(2,1)S(1)}, bf16[4,64,256]{2,1,0:T(8,128)(2,1)S(1)}, u32[]{:S(2)}, u32[]{:S(2)}) collective-permute-start(bf16[4,64,256]{2,1,0:T(8,128)(2,1)S(1)} %get-tuple-element.184), channel_id=1, source_target_pairs={{0,16},{8,24},{16,0},{24,8},{1,17},{9,25},{17,1},{25,9},{2,18},{10... | collective-permute-start | bytes 393224 | tf_op jit(solution)/shard_map/ppermute | solution.py:210
  34.0 9.3 %collective-permute-start.3 = (bf16[4,64,256]{2,1,0:T(8,128)(2,1)S(1)}, bf16[4,64,256]{2,1,0:T(8,128)(2,1)S(1)}, u32[]{:S(2)}, u32[]{:S(2)}) collective-permute-start(bf16[4,64,256]{2,1,0:T(8,128)(2,1)S(1)} %get-tuple-element.183), channel_id=1, source_target_pairs={{0,24},{8,0},{16,8},{24,16},{1,25},{9,1},{17,9},{25,17},{2,26},{10... | collective-permute-start | bytes 393224 | tf_op jit(solution)/shard_map/ppermute | solution.py:210
  44.3 3.2 %copy-start.7 = (bf16[256,256]{1,0:T(8,128)(2,1)S(1)}, bf16[256,256]{1,0:T(8,128)(2,1)}, u32[]{:S(2)}) copy-start(bf16[256,256]{1,0:T(8,128)(2,1)} %param.22) | copy-start | bytes 393220
  59.1 6.1 %copy-start.4 = (f32[64,4,16,16]{3,2,1,0:T(8,128)S(1)}, f32[64,4,16,16]{3,2,1,0:T(8,128)}, u32[]{:S(2)}) copy-start(f32[64,4,16,16]{3,2,1,0:T(8,128)} %fusion.52) | copy-start | bytes 786436
  81.4 1.8 %copy-start.9 = (bf16[256,256]{1,0:T(8,128)(2,1)S(1)}, bf16[256,256]{1,0:T(8,128)(2,1)}, u32[]{:S(2)}) copy-start(bf16[256,256]{1,0:T(8,128)(2,1)} %param.21) | copy-start | bytes 393220
  85.1 18.3 %all-to-all-start = ((bf16[16,64,256]{2,1,0:T(8,128)(2,1)}), bf16[16,64,256]{2,1,0:T(8,128)(2,1)S(1)}, u32[]{:S(2)}, u32[]{:S(2)}) async-start(bf16[16,64,256]{2,1,0:T(8,128)(2,1)} %bitcast.37), calls=%async_computation | async-start | bytes 1048576 | tf_op jit(solution)/shard_map/all_to_all | solution.py:219
  121.8 1.0 copy-start.6
  122.8 3.1 %collective-permute-start.5 = (f32[131072]{0:T(1024)S(1)}, f32[131072]{0:T(1024)S(1)}, u32[]{:S(2)}, u32[]{:S(2)}) collective-permute-start(f32[131072]{0:T(1024)S(1)} %broadcast_select_fusion), channel_id=1, source_target_pairs={{0,1},{1,0},{2,3},{3,2},{4,5},{5,4},{6,7},{7,6},{8,9},{9,8},{10,11... | collective-permute-start | bytes 1572872 | tf_op jit(solution)/shard_map/ppermute | solution.py:55
  126.0 31.7 %copy-start.11 = (bf16[4,128,256]{2,1,0:T(8,128)(2,1)S(1)}, bf16[4,128,256]{2,1,0:T(8,128)(2,1)}, u32[]{:S(2)}) copy-start(bf16[4,128,256]{2,1,0:T(8,128)(2,1)} %get-tuple-element.126) | copy-start | bytes 786436
  126.0 7.6 %collective-permute-start.6 = (f32[65536]{0:T(1024)S(1)}, f32[65536]{0:T(1024)S(1)}, u32[]{:S(2)}, u32[]{:S(2)}) collective-permute-start(f32[65536]{0:T(1024)S(1)} %slice_select_fusion), channel_id=1, source_target_pairs={{0,2},{1,3},{2,0},{3,1},{4,6},{5,7},{6,4},{7,5},{8,10},{9,11},{10,... | collective-permute-start | bytes 786440 | tf_op jit(solution)/shard_map/ppermute | solution.py:55
  127.3 45.2 %copy-start.10 = (s32[4,128]{1,0:T(4,128)S(1)}, s32[4,128]{1,0:T(4,128)}, u32[]{:S(2)}) copy-start(s32[4,128]{1,0:T(4,128)} %param.17) | copy-start | bytes 6148
  133.7 3.9 %collective-permute-start.7 = (f32[32768]{0:T(1024)S(1)}, f32[32768]{0:T(1024)S(1)}, u32[]{:S(2)}, u32[]{:S(2)}) collective-permute-start(f32[32768]{0:T(1024)S(1)} %slice_select_fusion.1), channel_id=1, source_target_pairs={{0,4},{1,5},{2,6},{3,7},{4,0},{5,1},{6,2},{7,3},{8,12},{9,13},{10,... | collective-permute-start | bytes 393224 | tf_op jit(solution)/shard_map/ppermute | solution.py:55
  137.6 3.2 %collective-permute-start.8 = (f32[16384]{0:T(1024)S(1)}, f32[16384]{0:T(1024)S(1)}, u32[]{:S(2)}, u32[]{:S(2)}) collective-permute-start(f32[16384]{0:T(1024)S(1)} %slice_select_fusion.2), channel_id=1, source_target_pairs={{0,8},{8,0},{16,24},{24,16},{1,9},{9,1},{17,25},{25,17},{2,10},{10... | collective-permute-start | bytes 196616 | tf_op jit(solution)/shard_map/ppermute | solution.py:55
  140.8 3.8 %collective-permute-start.9 = (f32[8192]{0:T(1024)S(1)}, f32[8192]{0:T(1024)S(1)}, u32[]{:S(2)}, u32[]{:S(2)}) collective-permute-start(f32[8192]{0:T(1024)S(1)} %slice_select_fusion.3), channel_id=1, source_target_pairs={{0,16},{8,24},{16,0},{24,8},{1,17},{9,25},{17,1},{25,9},{2,18},{10... | collective-permute-start | bytes 98312 | tf_op jit(solution)/shard_map/ppermute | solution.py:55
  144.6 4.7 %collective-permute-start.10 = (f32[8192]{0:T(1024)S(1)}, f32[8192]{0:T(1024)S(1)}, u32[]{:S(2)}, u32[]{:S(2)}) collective-permute-start(f32[8192]{0:T(1024)S(1)} %select_add_fusion.4), channel_id=1, source_target_pairs={{0,16},{8,24},{16,0},{24,8},{1,17},{9,25},{17,1},{25,9},{2,18},{10... | collective-permute-start | bytes 98312 | tf_op jit(solution)/shard_map/ppermute | solution.py:59
  149.3 3.2 %collective-permute-start.11 = (f32[16384]{0:T(1024)S(1)}, f32[16384]{0:T(1024)S(1)}, u32[]{:S(2)}, u32[]{:S(2)}) collective-permute-start(f32[16384]{0:T(1024)S(1)} %maximum_select_fusion.7), channel_id=1, source_target_pairs={{0,8},{8,0},{16,24},{24,16},{1,9},{9,1},{17,25},{25,17},{2,10},{10... | collective-permute-start | bytes 196616 | tf_op jit(solution)/shard_map/ppermute | solution.py:59
  152.5 3.9 %collective-permute-start.12 = (f32[32768]{0:T(1024)S(1)}, f32[32768]{0:T(1024)S(1)}, u32[]{:S(2)}, u32[]{:S(2)}) collective-permute-start(f32[32768]{0:T(1024)S(1)} %maximum_select_fusion.6), channel_id=1, source_target_pairs={{0,4},{1,5},{2,6},{3,7},{4,0},{5,1},{6,2},{7,3},{8,12},{9,13},{10,... | collective-permute-start | bytes 393224 | tf_op jit(solution)/shard_map/ppermute | solution.py:59
  156.4 9.1 %collective-permute-start.13 = (f32[65536]{0:T(1024)S(1)}, f32[65536]{0:T(1024)S(1)}, u32[]{:S(2)}, u32[]{:S(2)}) collective-permute-start(f32[65536]{0:T(1024)S(1)} %maximum_select_fusion.4), channel_id=1, source_target_pairs={{0,2},{1,3},{2,0},{3,1},{4,6},{5,7},{6,4},{7,5},{8,10},{9,11},{10,... | collective-permute-start | bytes 786440 | tf_op jit(solution)/shard_map/ppermute | solution.py:59
  157.6 14.8 %collective-permute-start.4 = (bf16[4,128,256]{2,1,0:T(8,128)(2,1)S(1)}, bf16[4,128,256]{2,1,0:T(8,128)(2,1)S(1)}, u32[]{:S(2)}, u32[]{:S(2)}) collective-permute-start(bf16[4,128,256]{2,1,0:T(8,128)(2,1)S(1)} %copy-done.11), channel_id=1, source_target_pairs={{0,7},{1,0},{2,1},{3,2},{4,3},{5,4},{6,5},{7,6},{8,15},{9,8},{10,9... | collective-permute-start | bytes 786440 | tf_op jit(solution)/shard_map/ppermute | solution.py:29
  165.5 8.7 %collective-permute-start.14 = (f32[131072]{0:T(1024)S(1)}, f32[131072]{0:T(1024)S(1)}, u32[]{:S(2)}, u32[]{:S(2)}) collective-permute-start(f32[131072]{0:T(1024)S(1)} %maximum_select_fusion.2), channel_id=1, source_target_pairs={{0,1},{1,0},{2,3},{3,2},{4,5},{5,4},{6,7},{7,6},{8,9},{9,8},{10,11... | collective-permute-start | bytes 1572872 | tf_op jit(solution)/shard_map/ppermute | solution.py:59
